TPU v7x, 32 devices: a whole 2x2x4 slice. The times are simulated.
32 devices in a mesh: chan: 8 (over z, y), tm: 4 (over x, core).
Axes of the slice: x: 2, y: 2, z: 4, core: 2. Of those that a mesh axis runs over, the one named last changes fastest.
Arguments:
- records: float32 [4, 3200, 512], P('tm', 'chan'), may hold values from -6 to 6
- chan_order: int32 [512], replicated, may hold values from 0 to 511, each once
- live_mask: int32 [512], replicated, may hold values 0 or 1
Outputs:
- stacks: float32 [2, 512, 64, 128], P(None, 'chan', 'tm')
Inputs may be any that keep to these rules, and one draw needn't show every extreme that they name: chan_order holds every channel number once.
All inputs are finite; a program needn't handle non-finite values.
Results may differ from a plain program's by a relative error of at most 0.0041.
Values may be sent and summed in bfloat16 or wider, within the bound.
No kernel may reach another device: no remote copies, remote signals or barrier semaphores. Data moves between devices by JAX's collectives and lax.ppermute only.
A program may use at most 64 MiB of HBM per device.

v0:
```python
import math
import jax
import jax.numpy as jnp
from jax import lax
from jax.sharding import PartitionSpec as P

L = 200
FB = 101
NLAG = 128
ROUNDS = 2
WIN_TM = 16


def shifted(block, axis, distance):
    devices = range(lax.axis_size(axis))
    route = [((i - distance) % len(devices), i) for i in devices]
    return lax.ppermute(block, axis, route)


def forward_table():
    sample_index = jnp.arange(L, dtype=jnp.int32)
    freq_index = jnp.arange(FB, dtype=jnp.int32)
    phase_step = jnp.mod(sample_index[:, None] * freq_index[None, :], L)
    phase_angle = phase_step.astype(jnp.float32) * (2.0 * math.pi / L)
    return jnp.concatenate([jnp.cos(phase_angle), -jnp.sin(phase_angle)], axis=1)


def smoothing_table():
    freq_index = jnp.arange(FB, dtype=jnp.int32)
    nearby = (jnp.abs(freq_index[:, None] - freq_index[None, :]) <= 2).astype(jnp.float32)
    return nearby / jnp.sum(nearby, axis=0, keepdims=True)


def inverse_table():
    freq_index = jnp.arange(FB, dtype=jnp.int32)
    lag_index = jnp.arange(NLAG, dtype=jnp.int32) - NLAG // 2
    phase_step = jnp.mod(freq_index[:, None] * lag_index[None, :], L)
    phase_angle = phase_step.astype(jnp.float32) * (2.0 * math.pi / L)
    edge = (freq_index == 0) | (freq_index == L // 2)
    fold_weight = jnp.where(edge, 1.0, 2.0).astype(jnp.float32) / L
    return jnp.stack(
        [fold_weight[:, None] * jnp.cos(phase_angle), -fold_weight[:, None] * jnp.sin(phase_angle)]
    )


def whiten_spectra(windows, live_block, precision=lax.Precision.HIGHEST):
    window_mean = jnp.mean(windows, axis=-2, keepdims=True)
    centred = windows - window_mean
    normed = centred / jnp.sqrt(jnp.mean(centred * centred, axis=-2, keepdims=True) + 1e-05)
    spectrum = jnp.einsum("...lk,lg->...kg", normed, forward_table(), precision=precision)
    real_part = spectrum[..., :FB]
    imag_part = spectrum[..., FB:]
    power = real_part * real_part + imag_part * imag_part
    smoothed = jnp.einsum("...f,fg->...g", power, smoothing_table(), precision=precision)
    mean_power = jnp.mean(power, axis=-1, keepdims=True)
    scale = live_block.astype(jnp.float32)[:, None] / jnp.sqrt(smoothed + 0.1 * mean_power + 1e-05)
    return jnp.concatenate([real_part * scale, imag_part * scale], axis=-1).astype(jnp.bfloat16)


def correlate(partner, own_spec, inverse):
    partner = partner.reshape(partner.shape[0], partner.shape[1], 2, FB)
    own_spec = own_spec.reshape(own_spec.shape[0], own_spec.shape[1], 2, FB)
    rotated = jnp.concatenate([own_spec[:, :, 1:2], -own_spec[:, :, 0:1]], axis=2)
    real_sum = jnp.einsum("wicf,wjcf->fji", partner, own_spec, preferred_element_type=jnp.float32)
    imag_sum = jnp.einsum("wicf,wjcf->fji", partner, rotated, preferred_element_type=jnp.float32)
    return jnp.einsum(
        "cfji,cfl->jil", jnp.stack([real_sum, imag_sum]), inverse, precision=lax.Precision.HIGHEST
    )


def on_device_reduce(records, chan_order, live_mask):
    chan_count = lax.axis_size("chan")
    position = lax.axis_index("chan")
    blocked = jnp.take(records, chan_order, axis=2)
    own_block = lax.all_to_all(blocked, "chan", split_axis=2, concat_axis=1, tiled=True)
    block_width = own_block.shape[2]
    own_windows = own_block.reshape(WIN_TM, L, block_width)
    live_blocks = jnp.take(live_mask, chan_order).reshape(chan_count, block_width)
    own_live = lax.dynamic_index_in_dim(live_blocks, position, 0, keepdims=False)
    own_spectra = whiten_spectra(own_windows, own_live)
    inverse = inverse_table()
    results = []
    for round_index in range(ROUNDS):
        offset = max(1, round_index * chan_count // 4)
        partner_block = shifted(own_windows, "chan", offset)
        source = jnp.mod(position - offset, chan_count)
        partner_live = lax.dynamic_index_in_dim(live_blocks, source, 0, keepdims=False)
        partner = whiten_spectra(partner_block, partner_live)
        lagged = correlate(partner, own_spectra, inverse)
        lagged = lax.psum_scatter(lagged, "tm", scatter_dimension=1, tiled=True)
        results.append(lagged)
    return jnp.stack(results)


def on_device_local(records, chan_order, live_mask):
    chan_count = lax.axis_size("chan")
    tm_count = lax.axis_size("tm")
    tm_position = lax.axis_index("tm")
    samples, channels = (records.shape[1], records.shape[2])
    block_width = channels // chan_count
    slice_width = block_width // tm_count
    windows = records.reshape(samples // L, L, channels)
    spectra = whiten_spectra(windows, live_mask, precision=lax.Precision.HIGH)
    spectra = jnp.take(spectra, chan_order, axis=1)
    own = lax.all_to_all(spectra, "chan", split_axis=1, concat_axis=0, tiled=True)
    gathered = lax.all_gather(own, "tm", axis=0, tiled=True)
    windows_all = gathered.shape[0]
    own_spec = gathered.reshape(windows_all, block_width, 2, FB)
    rotated = jnp.concatenate([own_spec[:, :, 1:2], -own_spec[:, :, 0:1]], axis=2)
    both = jnp.concatenate([own_spec, rotated], axis=1)
    my_slice = lax.dynamic_slice_in_dim(gathered, tm_position * slice_width, slice_width, axis=1)
    partners = []
    for round_index in range(ROUNDS):
        offset = max(1, round_index * chan_count // 4)
        partners.append(shifted(my_slice, "chan", offset))
    partner = jnp.concatenate(partners, axis=1).reshape(windows_all, ROUNDS * slice_width, 2, FB)
    sums = jnp.einsum("wicf,wjcf->fji", partner, both, preferred_element_type=jnp.float32)
    sums = sums.reshape(FB, 2, block_width, ROUNDS, slice_width)
    lagged = jnp.einsum("fcjri,cfl->rjil", sums, inverse_table(), precision=lax.Precision.HIGH)
    return lagged


def on_device(records, chan_order, live_mask):
    samples = records.shape[1]
    channels = records.shape[2]
    chan_count = lax.axis_size("chan")
    tm_count = lax.axis_size("tm")
    local_ok = (
        samples % L == 0
        and channels % chan_count == 0
        and (channels // chan_count % tm_count == 0)
        and (samples // L * chan_count == WIN_TM)
    )
    if local_ok:
        return on_device_local(records, chan_order, live_mask)
    return on_device_reduce(records, chan_order, live_mask)


def solution(mesh):
    placed = (P("tm", "chan", None), P(), P())
    return jax.shard_map(
        on_device,
        mesh=mesh,
        in_specs=placed,
        out_specs=P(None, "chan", "tm", None),
        check_vma=False,
    )
```

profile of v0, /device:TPU:4, one launch (start us, length us, event | category | flops | bytes accessed | tf_op | source)
XLA Modules:
  0.0 117.0 jit_solution(12994349782055250445)
XLA Ops:
  6.5 0.4 sine_negate_fusion
  7.0 0.1 convert_reduce_fusion
  7.1 0.7 compare_select_fusion
  7.8 0.7 compare_and_fusion
  8.5 1.2 %reduce_sum.36 = f32[2,512]{1,0:T(2,128)S(1)} reduce(f32[2,200,512]{2,1,0:T(8,128)} %bitcast.33, f32[]{:T(128)} %constant.41.clone.1), dimensions={1}, to_apply=%region_0.0 | reduce | flops 203776 | bytes 823300 | tf_op jit(solution)/shard_map/reduce_sum | solution.py:47
  9.7 1.3 %multiply_reduce_fusion = f32[2,512]{1,0:T(2,128)S(1)} fusion(f32[2,200,512]{2,1,0:T(8,128)} %bitcast.34, f32[2,512]{1,0:T(2,128)S(1)} %broadcast_multiply_fusion.1), kind=kLoop, calls=%fused_computation.18 | loop fusion | flops 613376 | bytes 827392 | tf_op jit(solution)/shard_map/reduce_sum | solution.py:49
  11.0 1.8 %fusion.12 = f32[2,512,202]{1,2,0:T(8,128)S(1)} fusion(f32[2,200,512]{2,1,0:T(8,128)} %bitcast.35, f32[2,512]{1,0:T(2,128)S(1)} %add_sqrt_fusion, f32[2,512]{1,0:T(2,128)S(1)} %broadcast_multiply_fusion.1, f32[200,101]{1,0:T(8,128)S(1)} %get-tuple-element.11, f32[200,101]{1,0:T(8,128)S(1)} %get-tuple-element.12), kind=kOutput, calls=%fused_computation.16 | convolution fusion | flops 248667600 | bytes 1816384 | tf_op jit(solution)/shard_map/...lk,lg->...kg/dot_general | solution.py:50
  12.8 0.1 fusion.28
  12.9 0.5 multiply_convert_fusion.1
  13.4 0.1 pad_maximum_fusion.1
  13.5 0.4 copy.16
  14.0 2.6 %gather_fusion = bf16[512,2,202]{2,1,0:T(2,128)(2,1)S(1)} fusion(bf16[2,512,202]{2,0,1:T(2,128)(2,1)S(1)} %copy.16, s32[1024]{0:T(1024)S(1)} %pad_clamp_fusion), kind=kCustom, calls=%fused_computation | custom fusion | bytes 829440 | tf_op jit(solution)/shard_map/jit(_take)/gather | solution.py:104
  16.5 1.8 %fusion.15 = bf16[2,512,202]{2,0,1:T(2,128)(2,1)S(1)} fusion(bf16[512,2,202]{2,1,0:T(2,128)(2,1)S(1)} %gather_fusion, pred[512]{0:T(512)(128)(4,1)S(1)} %compare_and_fusion), kind=kLoop, calls=%fused_computation.20 | loop fusion | flops 206848 | bytes 827904 | tf_op jit(solution)/shard_map/jit(_take)/select_n | solution.py:104
  18.4 20.1 %all_to_all.18 = bf16[2,512,202]{2,0,1:T(2,128)(2,1)S(1)} all-to-all(bf16[2,512,202]{2,0,1:T(2,128)(2,1)S(1)} %fusion.15), channel_id=1, replica_groups=mesh['chan'=8,'tm'=4] {'chan'}, dimensions={1} | all-to-all | bytes 827392 | tf_op jit(solution)/shard_map/all_to_all | solution.py:105
  38.4 0.1 copy.17
  38.5 0.8 copy.18
  39.4 21.7 %all-gather.2.cloned.1.call-done = bf16[64,64,202]{2,1,0:T(8,128)(2,1)} async-done(((bf16[16,64,202]{2,1,0:T(8,128)(2,1)}), bf16[64,64,202]{2,1,0:T(8,128)(2,1)}) %all-gather.2.cloned.1.call-update) | async-done | bytes 1654800 | tf_op jit(solution)/shard_map/all_gather | solution.py:106
  61.1 1.9 %constant_dynamic-slice_fusion = bf16[64,16,202]{2,1,0:T(8,128)(2,1)} fusion(bf16[64,64,202]{2,1,0:T(8,128)(2,1)} %all-gather.2.cloned.1.call-done, s32[]{:T(128)S(6)} %select_n.58), kind=kLoop, calls=%fused_computation.67 | loop fusion | bytes 827396 | tf_op jit(solution)/shard_map/dynamic_slice | solution.py:111
  63.0 1.5 %collective-permute-start = (bf16[64,16,202]{2,1,0:T(8,128)(2,1)}, bf16[64,16,202]{2,1,0:T(8,128)(2,1)}, u32[]{:S(2)}, u32[]{:S(2)}) collective-permute-start(bf16[64,16,202]{2,1,0:T(8,128)(2,1)} %constant_dynamic-slice_fusion), channel_id=1, source_target_pairs={{28,0},{0,4},{4,8},{8,12},{12,16},{16,20},{20,24},{24,28},{29,1},{... | collective-permute-start | bytes 1241096 | tf_op jit(solution)/shard_map/ppermute | solution.py:17
  64.5 1.5 %collective-permute-start.1 = (bf16[64,16,202]{2,1,0:T(8,128)(2,1)}, bf16[64,16,202]{2,1,0:T(8,128)(2,1)}, u32[]{:S(2)}, u32[]{:S(2)}) collective-permute-start(bf16[64,16,202]{2,1,0:T(8,128)(2,1)} %constant_dynamic-slice_fusion), channel_id=1, source_target_pairs={{24,0},{28,4},{0,8},{4,12},{8,16},{12,20},{16,24},{20,28},{25,1},{... | collective-permute-start | bytes 1241096 | tf_op jit(solution)/shard_map/ppermute | solution.py:17
  66.0 0.2 cosine_multiply_fusion
  66.2 4.3 %reshape.185 = bf16[64,64,2,101]{3,2,1,0:T(2,128)(2,1)} reshape(bf16[64,64,202]{2,1,0:T(8,128)(2,1)} %all-gather.2.cloned.1.call-done) | data formatting | bytes 3309568 | tf_op jit(solution)/shard_map/reshape | solution.py:108
  70.5 6.4 %copy.21 = bf16[64,64,2,101]{1,0,2,3:T(8,128)(2,1)S(1)} copy(bf16[64,64,2,101]{3,2,1,0:T(2,128)(2,1)} %reshape.185) | data formatting | bytes 3309568 | tf_op jit(solution)/shard_map/reshape | solution.py:108
  76.9 2.0 %fusion.44 = (bf16[64,64,1,101]{1,0,2,3:T(8,128)(2,1)}, bf16[64,64,1,101]{1,0,2,3:T(8,128)(2,1)}) fusion(bf16[64,64,2,101]{1,0,2,3:T(8,128)(2,1)S(1)} %copy.21), kind=kLoop, calls=%fused_computation.73 | loop fusion | flops 413696 | bytes 3309568 | tf_op jit(solution)/shard_map/slice | solution.py:109
  79.0 11.4 %collective-permute-done.1 = bf16[64,16,202]{2,1,0:T(8,128)(2,1)} collective-permute-done((bf16[64,16,202]{2,1,0:T(8,128)(2,1)}, bf16[64,16,202]{2,1,0:T(8,128)(2,1)}, u32[]{:S(2)}, u32[]{:S(2)}) %collective-permute-start.1) | collective-permute-done | bytes 413728 | tf_op jit(solution)/shard_map/ppermute | solution.py:17
  90.4 2.4 %pad_maximum_fusion = bf16[64,32,202]{2,1,0:T(8,128)(2,1)} fusion(bf16[64,16,202]{2,1,0:T(8,128)(2,1)} %collective-permute-done.1, bf16[64,16,202]{2,1,0:T(8,128)(2,1)} %collective-permute-done), kind=kLoop, calls=%fused_computation.14 | loop fusion | flops 1654784 | bytes 1654784 | tf_op jit(solution)/shard_map/concatenate | solution.py:116
  92.8 2.5 %reshape.186 = bf16[64,32,2,101]{3,2,1,0:T(2,128)(2,1)} reshape(bf16[64,32,202]{2,1,0:T(8,128)(2,1)} %pad_maximum_fusion) | data formatting | bytes 1654784 | tf_op jit(solution)/shard_map/reshape | solution.py:116
  95.3 4.5 %copy.22 = bf16[64,32,2,101]{0,1,2,3:T(8,128)(2,1)} copy(bf16[64,32,2,101]{3,2,1,0:T(2,128)(2,1)} %reshape.186) | data formatting | bytes 1654784 | tf_op jit(solution)/shard_map/reshape | solution.py:116
  99.8 5.8 %fusion.6 = f32[101,128,32]{1,2,0:T(8,128)} fusion(bf16[64,32,2,101]{0,1,2,3:T(8,128)(2,1)} %copy.22, bf16[64,64,1,101]{1,0,2,3:T(8,128)(2,1)} %get-tuple-element.6, bf16[64,64,1,101]{1,0,2,3:T(8,128)(2,1)} %get-tuple-element.5, bf16[64,64,2,101]{1,0,2,3:T(8,128)(2,1)S(1)} %copy.21), kind=kOutput, calls=%fused_computation.8 | convolution fusion | flops 115834880 | bytes 5791744 | tf_op jit(solution)/shard_map/wicf,wjcf->fji/dot_general | solution.py:117
  105.6 1.9 %copy.29 = f32[101,128,32]{0,1,2:T(8,128)S(1)} copy(f32[101,128,32]{1,2,0:T(8,128)} %fusion.6) | data formatting | bytes 3309568 | tf_op jit(solution)/shard_map/reshape | solution.py:118
  107.5 1.0 convolution_bitcast_fusion
  108.5 1.6 %copy.25 = f32[2,64,16,128]{3,2,1,0:T(8,128)} copy(f32[2,64,16,128]{3,1,2,0:T(8,128)S(1)} %convolution_bitcast_fusion) | data formatting | bytes 2097152 | tf_op jit(solution)/shard_map/fcjri,cfl->rjil/transpose | solution.py:119
  (12 shorter events, 0.1 us)
Async XLA Ops:
  6.5 54.6 %all-gather.2.cloned.1.call-start = ((), (), s32[]{:S(2)}) async-start(), calls=%async_computation.1 | async-start | bytes 2621440 | tf_op jit(solution)/shard_map/all_gather | solution.py:106
  11.0 1.9 %copy-start = (s32[512]{0:T(512)S(1)}, s32[512]{0:T(512)}, u32[]{:S(2)}) copy-start(s32[512]{0:T(512)} %param.5) | copy-start | bytes 6148
  63.0 16.0 %collective-permute-start = (bf16[64,16,202]{2,1,0:T(8,128)(2,1)}, bf16[64,16,202]{2,1,0:T(8,128)(2,1)}, u32[]{:S(2)}, u32[]{:S(2)}) collective-permute-start(bf16[64,16,202]{2,1,0:T(8,128)(2,1)} %constant_dynamic-slice_fusion), channel_id=1, source_target_pairs={{28,0},{0,4},{4,8},{8,12},{12,16},{16,20},{20,24},{24,28},{29,1},{... | collective-permute-start | bytes 1241096 | tf_op jit(solution)/shard_map/ppermute | solution.py:17
  64.5 25.9 %collective-permute-start.1 = (bf16[64,16,202]{2,1,0:T(8,128)(2,1)}, bf16[64,16,202]{2,1,0:T(8,128)(2,1)}, u32[]{:S(2)}, u32[]{:S(2)}) collective-permute-start(bf16[64,16,202]{2,1,0:T(8,128)(2,1)} %constant_dynamic-slice_fusion), channel_id=1, source_target_pairs={{24,0},{28,4},{0,8},{4,12},{8,16},{12,20},{16,24},{20,28},{25,1},{... | collective-permute-start | bytes 1241096 | tf_op jit(solution)/shard_map/ppermute | solution.py:17
Sparse Core Ops, SparseCore 0:
  39.5 21.6 all-gather.1
where the time goes:
time: 118 us; the launch traced here: 117 us
  waiting for transfers between devices  33.2 us (28%)
  local copies, waits for them, and re-layouts  27 us (23%)
  blocking collectives  20.1 us (17%)
  between operations  13.5 us (11%)
  other arithmetic  11.1 us (9%)
  matrix products  9.09 us (8%)
  starting transfers between devices  2.96 us (3%)
    all_gather x1, waiting for transfers between devices, on_device_local(): gathered = lax.all_gather(own, 'tm', axis=0, tiled=True)  21.7 us
    all_to_all x1, blocking collectives, on_device_local(): lax.all_to_all(spectra, 'chan', split_axis=1, concat_axis=0, tiled=True)  20.1 us
    ppermute x2, waiting for transfers between devices, shifted(): return lax.ppermute(block, axis, route)  11.4 us
    reshape x2, local copies, waits for them, and re-layouts, on_device_local(): own_spec = gathered.reshape(windows_all, block_width, 2, FB)  10.8 us
    reshape x2, local copies, waits for them, and re-layouts, on_device_local(): jnp.concatenate(partners, axis=1)  6.96 us
    dot_general x1, matrix products, on_device_local(): jnp.einsum('wicf,wjcf->fji', partner, both, preferred_element_type=jnp.fl...  5.77 us
    ppermute x2, starting transfers between devices, shifted(): return lax.ppermute(block, axis, route)  2.96 us
    gather x1, local copies, waits for them, and re-layouts, on_device_local(): spectra = jnp.take(spectra, chan_order, axis=1)  2.57 us
  transfers between devices with their start and end apart: 3, of which 2 were waited for; matrix products, arithmetic and copies ran while one was open for 11% of the time, Pallas kernels for 0%

commit v1 on v0

--- a/solution.py
+++ b/solution.py
@@ -102,7 +102,10 @@
     windows = records.reshape(samples // L, L, channels)
     spectra = whiten_spectra(windows, live_mask, precision=lax.Precision.HIGH)
     spectra = jnp.take(spectra, chan_order, axis=1)
-    own = lax.all_to_all(spectra, "chan", split_axis=1, concat_axis=0, tiled=True)
+    own = jnp.concatenate(
+        lax.all_to_all(jnp.stack(jnp.split(spectra, lax.axis_size("chan"), axis=1)), "chan", 0, 0),
+        axis=0,
+    )
     gathered = lax.all_gather(own, "tm", axis=0, tiled=True)
     windows_all = gathered.shape[0]
     own_spec = gathered.reshape(windows_all, block_width, 2, FB)

time: 118 us -> 118 us (level)
  no operation moved by 1% of the time
where the time goes in v1:
time: 118 us; the launch traced here: 117 us
  waiting for transfers between devices  33.2 us (28%)
  local copies, waits for them, and re-layouts  27.5 us (23%)
  blocking collectives  20.1 us (17%)
  between operations  13.6 us (12%)
  other arithmetic  11.1 us (9%)
  matrix products  9.09 us (8%)
  starting transfers between devices  2.96 us (3%)
    all_gather x1, waiting for transfers between devices, on_device_local(): gathered = lax.all_gather(own, 'tm', axis=0, tiled=True)  21.7 us
    all_to_all x1, blocking collectives, on_device_local(): lax.all_to_all(jnp.stack(jnp.split(spectra, lax.axis_size('chan'), axis=1...  20.1 us
    ppermute x2, waiting for transfers between devices, shifted(): return lax.ppermute(block, axis, route)  11.4 us
    reshape x2, local copies, waits for them, and re-layouts, on_device_local(): own_spec = gathered.reshape(windows_all, block_width, 2, FB)  10.8 us
    reshape x2, local copies, waits for them, and re-layouts, on_device_local(): jnp.concatenate(partners, axis=1)  6.96 us
    dot_general x1, matrix products, on_device_local(): jnp.einsum('wicf,wjcf->fji', partner, both, preferred_element_type=jnp.fl...  5.77 us
    ppermute x2, starting transfers between devices, shifted(): return lax.ppermute(block, axis, route)  2.96 us
    gather x1, local copies, waits for them, and re-layouts, on_device_local(): spectra = jnp.take(spectra, chan_order, axis=1)  2.57 us
  transfers between devices with their start and end apart: 3, of which 2 were waited for; matrix products, arithmetic and copies ran while one was open for 11% of the time, Pallas kernels for 0%

profile of v1, /device:TPU:4, one launch (start us, length us, event | category | flops | bytes accessed | tf_op | source)
XLA Modules:
  0.0 117.4 jit_solution(7977693875803705047)
XLA Ops:
  6.5 0.4 sine_negate_fusion
  7.0 0.1 convert_reduce_fusion
  7.1 0.7 compare_select_fusion
  7.8 0.7 compare_and_fusion
  8.5 1.2 %reduce_sum.36 = f32[2,512]{1,0:T(2,128)S(1)} reduce(f32[2,200,512]{2,1,0:T(8,128)} %bitcast.62, f32[]{:T(128)} %constant.41.clone.1), dimensions={1}, to_apply=%region_0.0 | reduce | flops 203776 | bytes 823300 | tf_op jit(solution)/shard_map/reduce_sum | solution.py:47
  9.7 1.3 %multiply_reduce_fusion = f32[2,512]{1,0:T(2,128)S(1)} fusion(f32[2,200,512]{2,1,0:T(8,128)} %bitcast.63, f32[2,512]{1,0:T(2,128)S(1)} %broadcast_multiply_fusion.1), kind=kLoop, calls=%fused_computation.18 | loop fusion | flops 613376 | bytes 827392 | tf_op jit(solution)/shard_map/reduce_sum | solution.py:49
  11.0 1.8 %fusion.12 = f32[2,512,202]{1,2,0:T(8,128)S(1)} fusion(f32[2,200,512]{2,1,0:T(8,128)} %bitcast.64, f32[2,512]{1,0:T(2,128)S(1)} %add_sqrt_fusion, f32[2,512]{1,0:T(2,128)S(1)} %broadcast_multiply_fusion.1, f32[200,101]{1,0:T(8,128)S(1)} %get-tuple-element.11, f32[200,101]{1,0:T(8,128)S(1)} %get-tuple-element.12), kind=kOutput, calls=%fused_computation.16 | convolution fusion | flops 248667600 | bytes 1816384 | tf_op jit(solution)/shard_map/...lk,lg->...kg/dot_general | solution.py:50
  12.8 0.1 fusion.28
  12.9 0.5 multiply_convert_fusion.1
  13.5 0.4 copy.23
  14.0 2.6 %gather_fusion = bf16[512,2,202]{2,1,0:T(2,128)(2,1)S(1)} fusion(bf16[2,512,202]{2,0,1:T(2,128)(2,1)S(1)} %copy.23, s32[1024]{0:T(1024)S(1)} %pad_clamp_fusion), kind=kCustom, calls=%fused_computation | custom fusion | bytes 829440 | tf_op jit(solution)/shard_map/jit(_take)/gather | solution.py:104
  16.5 1.8 %fusion.15 = bf16[2,512,202]{2,0,1:T(2,128)(2,1)S(1)} fusion(bf16[512,2,202]{2,1,0:T(2,128)(2,1)S(1)} %gather_fusion, pred[512]{0:T(512)(128)(4,1)S(1)} %compare_and_fusion), kind=kLoop, calls=%fused_computation.20 | loop fusion | flops 206848 | bytes 827904 | tf_op jit(solution)/shard_map/jit(_take)/select_n | solution.py:104
  18.4 0.1 fusion.35
  18.5 0.1 fusion.33
  18.8 20.1 %all_to_all.5 = bf16[8,2,64,202]{3,1,2,0:T(2,128)(2,1)S(1)} all-to-all(bf16[8,2,64,202]{3,1,2,0:T(2,128)(2,1)S(1)} %fusion.29), channel_id=1, replica_groups=mesh['chan'=8,'tm'=4] {'chan'}, dimensions={0} | all-to-all | bytes 827392 | tf_op jit(solution)/shard_map/all_to_all | solution.py:106
  38.9 0.9 copy.24
  39.8 21.7 %all-gather.2.cloned.1.call-done = bf16[64,64,202]{2,1,0:T(8,128)(2,1)} async-done(((bf16[16,64,202]{2,1,0:T(8,128)(2,1)}), bf16[64,64,202]{2,1,0:T(8,128)(2,1)}) %all-gather.2.cloned.1.call-update) | async-done | bytes 1654800 | tf_op jit(solution)/shard_map/all_gather | solution.py:109
  61.6 1.9 %constant_dynamic-slice_fusion = bf16[64,16,202]{2,1,0:T(8,128)(2,1)} fusion(bf16[64,64,202]{2,1,0:T(8,128)(2,1)} %all-gather.2.cloned.1.call-done, s32[]{:T(128)S(6)} %select_n.58), kind=kLoop, calls=%fused_computation.83 | loop fusion | bytes 827396 | tf_op jit(solution)/shard_map/dynamic_slice | solution.py:114
  63.5 1.5 %collective-permute-start = (bf16[64,16,202]{2,1,0:T(8,128)(2,1)}, bf16[64,16,202]{2,1,0:T(8,128)(2,1)}, u32[]{:S(2)}, u32[]{:S(2)}) collective-permute-start(bf16[64,16,202]{2,1,0:T(8,128)(2,1)} %constant_dynamic-slice_fusion), channel_id=1, source_target_pairs={{28,0},{0,4},{4,8},{8,12},{12,16},{16,20},{20,24},{24,28},{29,1},{... | collective-permute-start | bytes 1241096 | tf_op jit(solution)/shard_map/ppermute | solution.py:17
  64.9 1.5 %collective-permute-start.1 = (bf16[64,16,202]{2,1,0:T(8,128)(2,1)}, bf16[64,16,202]{2,1,0:T(8,128)(2,1)}, u32[]{:S(2)}, u32[]{:S(2)}) collective-permute-start(bf16[64,16,202]{2,1,0:T(8,128)(2,1)} %constant_dynamic-slice_fusion), channel_id=1, source_target_pairs={{24,0},{28,4},{0,8},{4,12},{8,16},{12,20},{16,24},{20,28},{25,1},{... | collective-permute-start | bytes 1241096 | tf_op jit(solution)/shard_map/ppermute | solution.py:17
  66.4 0.2 cosine_multiply_fusion
  66.7 4.3 %reshape.189 = bf16[64,64,2,101]{3,2,1,0:T(2,128)(2,1)} reshape(bf16[64,64,202]{2,1,0:T(8,128)(2,1)} %all-gather.2.cloned.1.call-done) | data formatting | bytes 3309568 | tf_op jit(solution)/shard_map/reshape | solution.py:111
  71.0 6.4 %copy.27 = bf16[64,64,2,101]{1,0,2,3:T(8,128)(2,1)S(1)} copy(bf16[64,64,2,101]{3,2,1,0:T(2,128)(2,1)} %reshape.189) | data formatting | bytes 3309568 | tf_op jit(solution)/shard_map/reshape | solution.py:111
  77.4 2.0 %fusion.52 = (bf16[64,64,1,101]{1,0,2,3:T(8,128)(2,1)}, bf16[64,64,1,101]{1,0,2,3:T(8,128)(2,1)}) fusion(bf16[64,64,2,101]{1,0,2,3:T(8,128)(2,1)S(1)} %copy.27), kind=kLoop, calls=%fused_computation.89 | loop fusion | flops 413696 | bytes 3309568 | tf_op jit(solution)/shard_map/slice | solution.py:112
  79.4 11.4 %collective-permute-done.1 = bf16[64,16,202]{2,1,0:T(8,128)(2,1)} collective-permute-done((bf16[64,16,202]{2,1,0:T(8,128)(2,1)}, bf16[64,16,202]{2,1,0:T(8,128)(2,1)}, u32[]{:S(2)}, u32[]{:S(2)}) %collective-permute-start.1) | collective-permute-done | bytes 413728 | tf_op jit(solution)/shard_map/ppermute | solution.py:17
  90.9 2.4 %pad_maximum_fusion = bf16[64,32,202]{2,1,0:T(8,128)(2,1)} fusion(bf16[64,16,202]{2,1,0:T(8,128)(2,1)} %collective-permute-done.1, bf16[64,16,202]{2,1,0:T(8,128)(2,1)} %collective-permute-done), kind=kLoop, calls=%fused_computation.14 | loop fusion | flops 1654784 | bytes 1654784 | tf_op jit(solution)/shard_map/concatenate | solution.py:119
  93.3 2.5 %reshape.190 = bf16[64,32,2,101]{3,2,1,0:T(2,128)(2,1)} reshape(bf16[64,32,202]{2,1,0:T(8,128)(2,1)} %pad_maximum_fusion) | data formatting | bytes 1654784 | tf_op jit(solution)/shard_map/reshape | solution.py:119
  95.8 4.5 %copy.28 = bf16[64,32,2,101]{0,1,2,3:T(8,128)(2,1)} copy(bf16[64,32,2,101]{3,2,1,0:T(2,128)(2,1)} %reshape.190) | data formatting | bytes 1654784 | tf_op jit(solution)/shard_map/reshape | solution.py:119
  100.3 5.8 %fusion.6 = f32[101,128,32]{1,2,0:T(8,128)} fusion(bf16[64,32,2,101]{0,1,2,3:T(8,128)(2,1)} %copy.28, bf16[64,64,1,101]{1,0,2,3:T(8,128)(2,1)} %get-tuple-element.6, bf16[64,64,1,101]{1,0,2,3:T(8,128)(2,1)} %get-tuple-element.5, bf16[64,64,2,101]{1,0,2,3:T(8,128)(2,1)S(1)} %copy.27), kind=kOutput, calls=%fused_computation.8 | convolution fusion | flops 115834880 | bytes 5791744 | tf_op jit(solution)/shard_map/wicf,wjcf->fji/dot_general | solution.py:120
  106.0 1.9 %copy.35 = f32[101,128,32]{0,1,2:T(8,128)S(1)} copy(f32[101,128,32]{1,2,0:T(8,128)} %fusion.6) | data formatting | bytes 3309568 | tf_op jit(solution)/shard_map/reshape | solution.py:121
  108.0 1.0 convolution_bitcast_fusion
  109.0 1.6 %copy.31 = f32[2,64,16,128]{3,2,1,0:T(8,128)} copy(f32[2,64,16,128]{3,1,2,0:T(8,128)S(1)} %convolution_bitcast_fusion) | data formatting | bytes 2097152 | tf_op jit(solution)/shard_map/fcjri,cfl->rjil/transpose | solution.py:122
  (19 shorter events, 0.5 us)
Async XLA Ops:
  6.5 55.0 %all-gather.2.cloned.1.call-start = ((), (), s32[]{:S(2)}) async-start(), calls=%async_computation.1 | async-start | bytes 2621440 | tf_op jit(solution)/shard_map/all_gather | solution.py:109
  11.0 1.9 %copy-start = (s32[512]{0:T(512)S(1)}, s32[512]{0:T(512)}, u32[]{:S(2)}) copy-start(s32[512]{0:T(512)} %param.5) | copy-start | bytes 6148
  63.5 16.0 %collective-permute-start = (bf16[64,16,202]{2,1,0:T(8,128)(2,1)}, bf16[64,16,202]{2,1,0:T(8,128)(2,1)}, u32[]{:S(2)}, u32[]{:S(2)}) collective-permute-start(bf16[64,16,202]{2,1,0:T(8,128)(2,1)} %constant_dynamic-slice_fusion), channel_id=1, source_target_pairs={{28,0},{0,4},{4,8},{8,12},{12,16},{16,20},{20,24},{24,28},{29,1},{... | collective-permute-start | bytes 1241096 | tf_op jit(solution)/shard_map/ppermute | solution.py:17
  64.9 25.9 %collective-permute-start.1 = (bf16[64,16,202]{2,1,0:T(8,128)(2,1)}, bf16[64,16,202]{2,1,0:T(8,128)(2,1)}, u32[]{:S(2)}, u32[]{:S(2)}) collective-permute-start(bf16[64,16,202]{2,1,0:T(8,128)(2,1)} %constant_dynamic-slice_fusion), channel_id=1, source_target_pairs={{24,0},{28,4},{0,8},{4,12},{8,16},{12,20},{16,24},{20,28},{25,1},{... | collective-permute-start | bytes 1241096 | tf_op jit(solution)/shard_map/ppermute | solution.py:17
Sparse Core Ops, SparseCore 0:
  39.9 21.6 all-gather.1
